TPU v7x, 32 devices: a whole 2x2x4 slice. The times are simulated.
32 devices in a mesh: well: 4 (over y, x), tile: 8 (over z, core).
Axes of the slice: x: 2, y: 2, z: 4, core: 2. Of those that a mesh axis runs over, the one named last changes fastest.
Arguments:
- prior_state: float32 [3, 200, 8192], P(None, None, 'tile'), may hold values from -6 to 6
- pred_data: float32 [4096, 200], P(('well', 'tile')), may hold values from -6 to 6
- obs_pert: float32 [4096, 200], P(('well', 'tile')), may hold values from -12 to 12
- obs_std: float32 [4096], P(('well', 'tile')), may hold values from 0.5 to 2
- loc_mask: int32 [8, 32], P('tile', 'well'), may hold values from 0 to 1, as said below
- taper_level: int32 [8, 32], P('tile', 'well'), may hold values from 1 to 4
Outputs:
- analysis: float32 [3, 200, 8192], P(None, 'well', 'tile')
Inputs may be any that keep to these rules, and one draw needn't show every extreme that they name: `loc_mask`: each tile is localized to a set of data blocks whose size varies strongly from tile to tile; some tile is localized to most blocks.
All inputs are finite; a program needn't handle non-finite values.
Results may differ from a plain program's by a relative error of at most 0.0003.
Values sent between devices are 32-bit elements; how exact they have to be, the bound alone decides.
No kernel may reach another device: no remote copies, remote signals or barrier semaphores. Data moves between devices by JAX's collectives and lax.ppermute only.
A program may use at most 64 MiB of HBM per device.

v0:
```python
import jax
import jax.numpy as jnp
from jax import lax
from jax.sharding import PartitionSpec as P

BLOCK = 128


def chol_apply(system, right):
    factor = jnp.linalg.cholesky(system)
    middle = lax.linalg.triangular_solve(
        factor, right, left_side=True, lower=True, transpose_a=False
    )
    return lax.linalg.triangular_solve(factor, middle, left_side=True, lower=True, transpose_a=True)


def prepare(pred_rows, obs_rows, std_rows, norm_factor):
    data_anom = (pred_rows - jnp.mean(pred_rows, axis=1, keepdims=True)) * norm_factor
    innov = obs_rows - pred_rows
    row_weight = 1.0 / (4.0 * std_rows * std_rows)
    scaled = row_weight[:, None] * data_anom
    return (data_anom, innov, row_weight, scaled)


def shards(prior_state, pred_data, obs_pert, obs_std, loc_mask, taper_level):
    highest = lax.Precision.HIGHEST
    members = pred_data.shape[1]
    norm_factor = 1.0 / jnp.sqrt(jnp.float32(members - 1))
    data_anom, innov, row_weight, scaled = prepare(pred_data, obs_pert, obs_std, norm_factor)
    gram_matrix, cross_matrix = lax.psum(
        (
            jnp.dot(data_anom.T, scaled, precision=highest),
            jnp.dot(scaled.T, innov, precision=highest),
        ),
        ("well", "tile"),
    )
    system = jnp.eye(members, dtype=jnp.float32) + gram_matrix
    solved = chol_apply(system, cross_matrix)
    gain_rows = row_weight[:, None] * innov - jnp.dot(scaled, solved, precision=highest)
    group_anom, group_gain = (
        lax.all_gather(data_anom, "tile", axis=0, tiled=True),
        lax.all_gather(gain_rows, "tile", axis=0, tiled=True),
    )
    taper_row = loc_mask[0].astype(jnp.float32) * taper_level[0].astype(jnp.float32) / 4.0
    state_anom = (prior_state - jnp.mean(prior_state, axis=1, keepdims=True)) * norm_factor
    own_count = members // lax.axis_size("well")
    own_start = lax.axis_index("well") * own_count
    row_taper = jnp.repeat(taper_row, BLOCK)
    space = jnp.dot((group_anom * row_taper[:, None]).T, group_gain, precision=highest)
    space_mine = lax.psum_scatter(space, "well", scatter_dimension=1, tiled=True)
    increment = jnp.einsum("vnc,nm->vmc", state_anom, space_mine, precision=highest)
    prior_mine = lax.dynamic_slice_in_dim(prior_state, own_start, own_count, 1)
    return prior_mine + increment


def solution(mesh):
    return jax.shard_map(
        shards,
        mesh=mesh,
        in_specs=(
            P(None, None, "tile"),
            P(("well", "tile"), None),
            P(("well", "tile"), None),
            P(("well", "tile")),
            P("tile", "well"),
            P("tile", "well"),
        ),
        out_specs=P(None, "well", "tile"),
        check_vma=False,
    )
```

profile of v0, /device:TPU:4, one launch (start us, length us, event | category | flops | bytes accessed | tf_op | source)
XLA Modules:
  0.0 278.2 jit_solution(14750965140446197229)
XLA Ops:
  6.5 0.0 copy-start.9
  6.5 0.0 copy-start.8
  6.5 0.0 copy-start
  6.5 0.0 all-reduce.8.cloned.1.call-start
  6.5 1.1 reduce_sum.18
  7.6 1.2 broadcast_multiply_fusion.1
  8.8 0.0 copy-start.6
  8.8 2.0 fusion.22
  10.8 0.0 copy-done.6
  10.8 2.0 fusion.21
  12.8 0.0 all-reduce.8.cloned.1.call-update
  12.9 0.9 subtract_multiply_fusion.1
  13.8 16.0 %all_gather.6 = f32[1024,200]{0,1:T(8,128)S(1)} all-gather(f32[128,200]{0,1:T(8,128)S(1)} %subtract_multiply_fusion.1), channel_id=1, replica_groups=mesh['well'=4,'tile'=8] {'tile'}, dimensions={0}, use_global_device_ids=true | all-gather | bytes 921600 | tf_op jit(solution)/shard_map/all_gather | solution.py:41
  29.8 0.0 copy-done.9
  29.8 0.0 copy-done.8
  29.8 0.1 broadcast_bitcast_fusion
  29.9 0.0 copy-done
  29.9 0.8 reduce_sum.19
  30.6 110.1 %all-reduce.8.cloned.1.call-done = (f32[200,200]{1,0:T(8,128)}, f32[200,200]{0,1:T(8,128)}) async-done(((f32[200,200]{1,0:T(8,128)}, f32[200,200]{0,1:T(8,128)}), (f32[200,200]{1,0:T(8,128)}, f32[200,200]{0,1:T(8,128)})) %all-reduce.8.cloned.1.call-update) | async-done | bytes 320016 | tf_op jit(solution)/shard_map/psum | solution.py:30
  140.7 0.0 copy-start.1
  140.7 0.0 copy-start.4
  140.7 1.7 convert_add_fusion
  142.4 1.7 copy.10
  144.1 1.1 fusion.18
  145.2 0.0 copy-start.3
  145.2 0.7 copy-done.3
  145.9 0.6 cholesky.124
  146.5 13.2 %cholesky.51 = f32[128,128]{1,0:T(8,128)} custom-call(f32[128,128]{1,0:T(8,128)} %cholesky.124), custom_call_target="Cholesky" | custom-call | tf_op jit(solution)/shard_map/jit(cholesky)/cholesky | solution.py:10
  159.7 2.0 select_reduce_fusion
  161.7 1.5 cholesky.119
  163.2 11.3 %custom-call.16 = f32[1,128,128]{1,2,0:T(8,128)} custom-call(f32[1,128,128]{2,1,0:T(8,128)} %get-tuple-element.30), custom_call_target="InvertDiagBlocksLowerTriangular" | custom-call | tf_op jit(solution)/shard_map/jit(cholesky)/cholesky | solution.py:10
  174.5 1.7 constant_dynamic-update-slice_fusion.1
  176.2 1.6 convolution_subtract_fusion.3
  177.8 8.0 %cholesky.110 = f32[72,72]{1,0:T(8,128)} custom-call(f32[72,72]{1,0:T(8,128)} %convolution_subtract_fusion.3), custom_call_target="Cholesky" | custom-call | tf_op jit(solution)/shard_map/jit(cholesky)/cholesky | solution.py:10
  185.7 1.4 select_reduce_fusion.1
  187.1 0.6 compare_reduce_fusion
  187.8 1.3 compare_reduce_fusion.1
  190.3 1.0 select_select_fusion
  191.2 0.0 copy-start.2
  191.3 0.7 copy-done.2
  191.9 0.1 fusion.23
  192.0 0.7 pad_maximum_fusion
  192.7 21.1 %custom-call.17 = f32[2,128,128]{1,2,0:T(8,128)} custom-call(f32[2,128,128]{2,1,0:T(8,128)} %pad_maximum_fusion), custom_call_target="InvertDiagBlocksLowerTriangular" | custom-call | tf_op jit(solution)/shard_map/triangular_solve | solution.py:14
  213.8 1.4 fusion.19
  215.1 0.0 copy-start.5
  215.1 0.0 copy-start.7
  215.2 1.2 convolution_subtract_fusion.2
  216.4 1.0 fusion.36
  217.4 1.0 fusion.35
  218.4 1.1 convolution_subtract_fusion
  219.6 1.2 fusion.26
  220.8 0.0 copy-done.1
  220.8 0.0 copy-done.4
  220.8 1.2 convolution_subtract_fusion.1
  222.0 17.3 %all_gather.7 = f32[1024,200]{0,1:T(8,128)S(1)} all-gather(f32[128,200]{0,1:T(8,128)S(1)} %convolution_subtract_fusion.1), channel_id=1, replica_groups=mesh['well'=4,'tile'=8] {'tile'}, dimensions={0}, use_global_device_ids=true | all-gather | bytes 921600 | tf_op jit(solution)/shard_map/all_gather | solution.py:42
  239.3 0.9 fusion.12
  240.2 21.4 %fusion = f32[200,64]{0,1:T(8,128)S(1)} fusion(f32[200,200]{0,1:T(8,128)S(1)} %fusion.12), kind=kCustom, calls=%all-reduce-scatter | all-reduce-scatter fusion | flops 51201 | bytes 211712
  261.7 3.4 %collective-permute-start = (f32[200,42]{0,1:T(8,128)S(1)}, f32[200,42]{0,1:T(8,128)S(1)}, u32[]{:S(2)}, u32[]{:S(2)}) collective-permute-start(f32[200,42]{0,1:T(8,128)S(1)} %slice.74), channel_id=1, source_target_pairs={{0,8},{8,16},{16,24},{1,9},{9,17},{17,25},{2,10},{10,18},{18,26},{... | collective-permute-start | bytes 100808
  265.0 0.0 copy-done.5
  265.1 0.0 copy-done.7
  265.1 0.6 dynamic-slice.8
  266.3 2.2 collective-permute-done
  268.5 0.2 concatenate.13
  268.7 2.6 fusion.7
  (7 shorter events, 0.0 us)
Async XLA Ops:
  6.5 23.3 %copy-start.9 = (s32[1,8]{1,0:T(1,128)S(1)}, s32[1,8]{1,0:T(1,128)}, u32[]{:S(2)}) copy-start(s32[1,8]{1,0:T(1,128)} %param.10) | copy-start | bytes 100
  6.5 23.3 %copy-start.8 = (s32[1,8]{1,0:T(1,128)S(1)}, s32[1,8]{1,0:T(1,128)}, u32[]{:S(2)}) copy-start(s32[1,8]{1,0:T(1,128)} %param.11) | copy-start | bytes 100
  6.5 23.3 %copy-start = (f32[3,200,1024]{2,1,0:T(8,128)S(1)}, f32[3,200,1024]{2,1,0:T(8,128)}, u32[]{:S(2)}) copy-start(f32[3,200,1024]{2,1,0:T(8,128)} %param.6) | copy-start | bytes 7372804
  6.5 134.2 %all-reduce.8.cloned.1.call-start = ((), (), s32[]{:S(2)}) async-start(), calls=%async_computation | async-start | bytes 819200 | tf_op jit(solution)/shard_map/psum | solution.py:30
  8.8 2.0 copy-start.6
  140.7 80.0 %copy-start.1 = (f32[128,200]{0,1:T(8,128)S(1)}, f32[128,200]{0,1:T(8,128)}, u32[]{:S(2)}) copy-start(f32[128,200]{0,1:T(8,128)} %param.7) | copy-start | bytes 307204
  140.7 80.0 %copy-start.4 = (f32[128,200]{0,1:T(8,128)S(1)}, f32[128,200]{0,1:T(8,128)}, u32[]{:S(2)}) copy-start(f32[128,200]{0,1:T(8,128)} %param.8) | copy-start | bytes 307204
  145.2 0.7 copy-start.3
  191.2 0.7 copy-start.2
  215.1 49.9 %copy-start.5 = (f32[3,1024]{1,0:T(4,128)S(1)}, f32[3,1024]{1,0:T(4,128)}, u32[]{:S(2)}) copy-start(f32[3,1024]{1,0:T(4,128)} %reduce_sum.19) | copy-start | bytes 36868
  215.1 49.9 %copy-start.7 = (u32[32]{0:T(128)S(1)}, u32[32]{0:T(128)}, u32[]{:S(2)}) copy-start(u32[32]{0:T(128)} %constant.155) | copy-start | bytes 388
  261.7 6.9 %collective-permute-start = (f32[200,42]{0,1:T(8,128)S(1)}, f32[200,42]{0,1:T(8,128)S(1)}, u32[]{:S(2)}, u32[]{:S(2)}) collective-permute-start(f32[200,42]{0,1:T(8,128)S(1)} %slice.74), channel_id=1, source_target_pairs={{0,8},{8,16},{16,24},{1,9},{9,17},{17,25},{2,10},{10,18},{18,26},{... | collective-permute-start | bytes 100808
Sparse Core Ops, SparseCore 0:
  13.0 127.6 all-reduce.7
where the time goes:
time: 279 us; the launch traced here: 278 us
  waiting for transfers between devices  112 us (40%)
  other arithmetic  67.3 us (24%)
  blocking collectives  54.7 us (20%)
  matrix products  19 us (7%)
  between operations  15.4 us (6%)
  local copies, waits for them, and re-layouts  6.12 us (2%)
  starting transfers between devices  3.37 us (1%)
    psum x1, waiting for transfers between devices, shards(): lax.psum((jnp.dot(data_anom.T, scaled, precision=highest), jnp.dot(scaled...  110 us
    another operation x7, other arithmetic, chol_apply(): factor = jnp.linalg.cholesky(system)  37.8 us
    another operation x6, other arithmetic, chol_apply(): lax.linalg.triangular_solve(factor, middle, left_side=True, lower=True, t...  22.8 us
    unnamed x1, blocking collectives  21.4 us
    all_gather x1, blocking collectives, shards(): lax.all_gather(gain_rows, 'tile', axis=0, tiled=True)  17.3 us
    all_gather x1, blocking collectives, shards(): lax.all_gather(data_anom, 'tile', axis=0, tiled=True)  16 us
  transfers between devices with their start and end apart: 2, of which 2 were waited for; matrix products, arithmetic and copies ran while one was open for 1% of the time, Pallas kernels for 0%

commit v1 on v0

--- a/solution.py
+++ b/solution.py
@@ -4,6 +4,19 @@
 from jax.sharding import PartitionSpec as P
 
 BLOCK = 128
+
+
+def gather_around(shard, axis, dim):
+    ways = lax.axis_size(axis)
+    up = [(d, (d + 1) % ways) for d in range(ways)]
+    down = [(d, (d - 1) % ways) for d in range(ways)]
+    earlier, later = ([shard], [shard])
+    for _ in range(ways // 2):
+        earlier.append(lax.ppermute(earlier[-1], axis, up))
+    for _ in range((ways - 1) // 2):
+        later.append(lax.ppermute(later[-1], axis, down))
+    line = jnp.concatenate([*earlier[::-1], *later[1:]], axis=dim)
+    return jnp.roll(line, (lax.axis_index(axis) - ways // 2) * shard.shape[dim], axis=dim)
 
 
 def chol_apply(system, right):
@@ -38,7 +51,7 @@
     solved = chol_apply(system, cross_matrix)
     gain_rows = row_weight[:, None] * innov - jnp.dot(scaled, solved, precision=highest)
     group_anom, group_gain = (
-        lax.all_gather(data_anom, "tile", axis=0, tiled=True),
+        gather_around(data_anom, "tile", 0),
         lax.all_gather(gain_rows, "tile", axis=0, tiled=True),
     )
     taper_row = loc_mask[0].astype(jnp.float32) * taper_level[0].astype(jnp.float32) / 4.0

time: 279 us -> 265 us (0.950)
  waiting for transfers between devices: 112 us -> 130 us
  blocking collectives: 54.7 us -> 38.6 us
  other arithmetic: 67.3 us -> 55.6 us
  starting transfers between devices: 3.37 us -> 12.8 us
  matrix products: 19 us -> 10.5 us
  local copies, waits for them, and re-layouts: 6.12 us -> 1.16 us
    all_gather x1 -> x0, blocking collectives: 16 us -> none  [shards(): lax.all_gather(data_anom, 'tile', axis=0, tiled=True)]
    psum x1, waiting for transfers between devices: 110 us -> 120 us  [shards(): lax.psum((jnp.dot(data_anom.T, scaled, precision=highest), jnp.dot(scaled...]
    ppermute x0 -> x7, starting transfers between devices: none -> 9.46 us  [the longest x3 9.29 us: gather_around(): later.append(lax.ppermute(later[-1], axis, down))]
    another operation x7, other arithmetic: 37.8 us -> 29.4 us  [chol_apply(): factor = jnp.linalg.cholesky(system)]
    ppermute x0 -> x7, waiting for transfers between devices: none -> 7.41 us  [the longest x4 5.27 us: gather_around(): earlier.append(lax.ppermute(earlier[-1], axis, up))]
    another operation x6, other arithmetic: 22.8 us -> 19.8 us  [chol_apply(): lax.linalg.triangular_solve(factor, middle, left_side=True, lower=True, t...]
    another operation x2, matrix products: 3.27 us -> 0.42 us  [chol_apply(): factor = jnp.linalg.cholesky(system)]
  transfers between devices with their start and end apart: 2 -> 9, of which waited for: 2 -> 4; matrix products, arithmetic and copies ran while one was open for 1% -> 23% of each run, Pallas kernels for 0% -> 0%
where the time goes in v1:
time: 265 us; the launch traced here: 264 us
  waiting for transfers between devices  130 us (49%)
  other arithmetic  55.6 us (21%)
  blocking collectives  38.6 us (15%)
  between operations  15.7 us (6%)
  starting transfers between devices  12.8 us (5%)
  matrix products  10.5 us (4%)
    psum x1, waiting for transfers between devices, shards(): lax.psum((jnp.dot(data_anom.T, scaled, precision=highest), jnp.dot(scaled...  120 us
    another operation x7, other arithmetic, chol_apply(): factor = jnp.linalg.cholesky(system)  29.4 us
    unnamed x1, blocking collectives  22.3 us
    another operation x6, other arithmetic, chol_apply(): lax.linalg.triangular_solve(factor, middle, left_side=True, lower=True, t...  19.8 us
    all_gather x1, blocking collectives, shards(): lax.all_gather(gain_rows, 'tile', axis=0, tiled=True)  16.3 us
    ppermute x3, starting transfers between devices, gather_around(): later.append(lax.ppermute(later[-1], axis, down))  9.29 us
  transfers between devices with their start and end apart: 9, of which 4 were waited for; matrix products, arithmetic and copies ran while one was open for 23% of the time, Pallas kernels for 0%

profile of v1, /device:TPU:4, one launch (start us, length us, event | category | flops | bytes accessed | tf_op | source)
XLA Modules:
  0.0 264.3 jit_solution(15353540061912875549)
XLA Ops:
  6.5 0.0 copy-start.6
  6.5 0.0 copy-start.5
  6.5 0.0 all-reduce.8.cloned.1.call-start
  6.5 1.0 reduce_sum.18
  7.5 0.7 broadcast_multiply_fusion.1
  8.2 0.9 subtract_multiply_fusion.1
  9.1 0.1 collective-permute-start
  9.1 3.5 %collective-permute-start.4 = (f32[128,200]{0,1:T(8,128)S(1)}, f32[128,200]{0,1:T(8,128)S(1)}, u32[]{:S(2)}, u32[]{:S(2)}) collective-permute-start(f32[128,200]{0,1:T(8,128)S(1)} %subtract_multiply_fusion.1), channel_id=1, source_target_pairs={{0,7},{1,0},{2,1},{3,2},{4,3},{5,4},{6,5},{7,6},{8,15},{9,8},{10,9... | collective-permute-start | bytes 307208 | tf_op jit(solution)/shard_map/ppermute | solution.py:17
  12.7 2.0 fusion.23
  14.7 2.0 fusion.22
  16.7 0.0 all-reduce.8.cloned.1.call-update
  16.7 0.0 copy-done.6
  16.7 0.0 copy-done.5
  16.8 0.1 broadcast_bitcast_fusion
  16.8 1.9 reduce_sum.19
  18.7 0.0 collective-permute-done
  18.7 0.1 collective-permute-start.1
  18.8 0.0 collective-permute-done.4
  18.8 3.5 %collective-permute-start.5 = (f32[128,200]{0,1:T(8,128)S(1)}, f32[128,200]{0,1:T(8,128)S(1)}, u32[]{:S(2)}, u32[]{:S(2)}) collective-permute-start(f32[128,200]{0,1:T(8,128)S(1)} %collective-permute-done.4), channel_id=1, source_target_pairs={{0,7},{1,0},{2,1},{3,2},{4,3},{5,4},{6,5},{7,6},{8,15},{9,8},{10,9... | collective-permute-start | bytes 307208 | tf_op jit(solution)/shard_map/ppermute | solution.py:17
  22.3 120.2 %all-reduce.8.cloned.1.call-done = (f32[200,200]{1,0:T(8,128)}, f32[200,200]{0,1:T(8,128)}) async-done(((f32[200,200]{1,0:T(8,128)}, f32[200,200]{0,1:T(8,128)}), (f32[200,200]{1,0:T(8,128)}, f32[200,200]{0,1:T(8,128)})) %all-reduce.8.cloned.1.call-update) | async-done | bytes 320016 | tf_op jit(solution)/shard_map/psum | solution.py:43
  142.6 0.0 copy-start.3
  142.6 1.0 convert_add_fusion
  143.6 0.1 copy.10
  143.7 1.0 fusion.19
  144.7 11.7 %cholesky.51 = f32[128,128]{1,0:T(8,128)S(1)} custom-call(f32[128,128]{1,0:T(8,128)S(1)} %cholesky.124), custom_call_target="Cholesky" | custom-call | tf_op jit(solution)/shard_map/jit(cholesky)/cholesky | solution.py:23
  156.4 0.0 copy-start.2
  156.5 9.8 %custom-call.16 = f32[1,128,128]{1,2,0:T(8,128)S(1)} custom-call(f32[1,128,128]{2,1,0:T(8,128)S(1)} %get-tuple-element.30), custom_call_target="InvertDiagBlocksLowerTriangular" | custom-call | tf_op jit(solution)/shard_map/jit(cholesky)/cholesky | solution.py:23
  166.3 0.2 constant_dynamic-update-slice_fusion.16
  166.5 0.2 convolution_subtract_fusion.3
  166.7 6.6 %cholesky.110 = f32[72,72]{1,0:T(8,128)S(1)} custom-call(f32[72,72]{1,0:T(8,128)S(1)} %convolution_subtract_fusion.3), custom_call_target="Cholesky" | custom-call | tf_op jit(solution)/shard_map/jit(cholesky)/cholesky | solution.py:23
  173.3 0.6 compare_reduce_fusion
  174.0 0.6 compare_reduce_fusion.1
  175.9 0.1 fusion.24
  176.0 19.7 %custom-call.17 = f32[2,128,128]{1,2,0:T(8,128)S(1)} custom-call(f32[2,128,128]{2,1,0:T(8,128)S(1)} %pad_maximum_fusion), custom_call_target="InvertDiagBlocksLowerTriangular" | custom-call | tf_op jit(solution)/shard_map/triangular_solve | solution.py:27
  195.7 0.0 copy-done.3
  195.7 0.4 fusion.20
  196.1 0.3 convolution_subtract_fusion.2
  196.4 0.3 fusion.37
  196.7 0.2 fusion.36
  196.9 0.4 convolution_subtract_fusion
  197.3 0.3 fusion.27
  197.6 0.0 collective-permute-done.1
  197.6 0.1 collective-permute-start.2
  197.7 0.0 copy-done.1
  197.7 0.0 copy-done.2
  197.7 0.6 convolution_subtract_fusion.1
  198.3 5.3 %collective-permute-done.2 = f32[128,200]{0,1:T(8,128)S(1)} collective-permute-done((f32[128,200]{0,1:T(8,128)S(1)}, f32[128,200]{0,1:T(8,128)S(1)}, u32[]{:S(2)}, u32[]{:S(2)}) %collective-permute-start.2) | collective-permute-done | bytes 102432 | tf_op jit(solution)/shard_map/ppermute | solution.py:15
  203.6 0.0 collective-permute-start.3
  203.6 16.3 %all_gather.3 = f32[1024,200]{0,1:T(8,128)S(1)} all-gather(f32[128,200]{0,1:T(8,128)S(1)} %convolution_subtract_fusion.1), channel_id=1, replica_groups=mesh['well'=4,'tile'=8] {'tile'}, dimensions={0}, use_global_device_ids=true | all-gather | bytes 921600 | tf_op jit(solution)/shard_map/all_gather | solution.py:55
  219.9 0.0 collective-permute-done.5
  219.9 2.2 collective-permute-start.6
  222.2 0.0 collective-permute-done.3
  222.3 2.1 collective-permute-done.6
  224.5 0.0 copy-start.4
  224.5 0.0 copy-start
  224.6 0.9 fusion.12
  225.5 22.3 %fusion = f32[200,64]{0,1:T(8,128)S(1)} fusion(f32[200,200]{0,1:T(8,128)S(1)} %fusion.12), kind=kCustom, calls=%all-reduce-scatter | all-reduce-scatter fusion | flops 51201 | bytes 211712
  247.8 3.4 %collective-permute-start.7 = (f32[200,42]{0,1:T(8,128)S(1)}, f32[200,42]{0,1:T(8,128)S(1)}, u32[]{:S(2)}, u32[]{:S(2)}) collective-permute-start(f32[200,42]{0,1:T(8,128)S(1)} %slice.74), channel_id=1, source_target_pairs={{0,8},{8,16},{16,24},{1,9},{9,17},{17,25},{2,10},{10,18},{18,26},{... | collective-permute-start | bytes 100808
  251.2 0.0 copy-done.4
  251.2 0.6 dynamic-slice.8
  252.4 2.2 collective-permute-done.7
  254.6 0.2 concatenate.20
  254.8 0.0 copy-done
  254.9 2.6 %fusion.7 = f32[3,50,1024]{2,1,0:T(8,128)} fusion(f32[3,200,1024]{2,1,0:T(8,128)S(1)} %copy-done, f32[3,1024]{1,0:T(4,128)S(1)} %broadcast_multiply_fusion, s32[]{:T(128)S(6)} %select_n.20, f32[200,106]{0,1:T(8,128)S(1)} %concatenate.20, u32[]{:S(6)} %subtract.8), kind=kOutput, calls=%fused_computation.4 | convolution fusion | flops 370022400 | bytes 3833864 | tf_op jit(solution)/shard_map/vnc,nm->vmc/dot_general | solution.py:64
  (30 shorter events, 0.3 us)
Async XLA Ops:
  6.5 10.2 %copy-start.6 = (s32[1,8]{1,0:T(1,128)S(1)}, s32[1,8]{1,0:T(1,128)}, u32[]{:S(2)}) copy-start(s32[1,8]{1,0:T(1,128)} %param.10) | copy-start | bytes 100
  6.5 10.2 %copy-start.5 = (s32[1,8]{1,0:T(1,128)S(1)}, s32[1,8]{1,0:T(1,128)}, u32[]{:S(2)}) copy-start(s32[1,8]{1,0:T(1,128)} %param.11) | copy-start | bytes 100
  6.5 136.0 %all-reduce.8.cloned.1.call-start = ((), (), s32[]{:S(2)}) async-start(), calls=%async_computation | async-start | bytes 819200 | tf_op jit(solution)/shard_map/psum | solution.py:43
  9.1 9.7 %collective-permute-start = (f32[128,200]{0,1:T(8,128)S(1)}, f32[128,200]{0,1:T(8,128)S(1)}, u32[]{:S(2)}, u32[]{:S(2)}) collective-permute-start(f32[128,200]{0,1:T(8,128)S(1)} %subtract_multiply_fusion.1), channel_id=1, source_target_pairs={{0,1},{1,2},{2,3},{3,4},{4,5},{5,6},{6,7},{7,0},{8,9},{9,10},{10,1... | collective-permute-start | bytes 307208 | tf_op jit(solution)/shard_map/ppermute | solution.py:15
  9.1 9.7 %collective-permute-start.4 = (f32[128,200]{0,1:T(8,128)S(1)}, f32[128,200]{0,1:T(8,128)S(1)}, u32[]{:S(2)}, u32[]{:S(2)}) collective-permute-start(f32[128,200]{0,1:T(8,128)S(1)} %subtract_multiply_fusion.1), channel_id=1, source_target_pairs={{0,7},{1,0},{2,1},{3,2},{4,3},{5,4},{6,5},{7,6},{8,15},{9,8},{10,9... | collective-permute-start | bytes 307208 | tf_op jit(solution)/shard_map/ppermute | solution.py:17
  18.7 178.9 %collective-permute-start.1 = (f32[128,200]{0,1:T(8,128)S(1)}, f32[128,200]{0,1:T(8,128)S(1)}, u32[]{:S(2)}, u32[]{:S(2)}) collective-permute-start(f32[128,200]{0,1:T(8,128)S(1)} %collective-permute-done), channel_id=1, source_target_pairs={{0,1},{1,2},{2,3},{3,4},{4,5},{5,6},{6,7},{7,0},{8,9},{9,10},{10,1... | collective-permute-start | bytes 307208 | tf_op jit(solution)/shard_map/ppermute | solution.py:15
  18.8 201.1 %collective-permute-start.5 = (f32[128,200]{0,1:T(8,128)S(1)}, f32[128,200]{0,1:T(8,128)S(1)}, u32[]{:S(2)}, u32[]{:S(2)}) collective-permute-start(f32[128,200]{0,1:T(8,128)S(1)} %collective-permute-done.4), channel_id=1, source_target_pairs={{0,7},{1,0},{2,1},{3,2},{4,3},{5,4},{6,5},{7,6},{8,15},{9,8},{10,9... | collective-permute-start | bytes 307208 | tf_op jit(solution)/shard_map/ppermute | solution.py:17
  142.6 53.1 %copy-start.3 = (f32[200,200]{1,0:T(8,128)S(1)}, f32[200,200]{1,0:T(8,128)}, u32[]{:S(2)}) copy-start(f32[200,200]{1,0:T(8,128)} %get-tuple-element.25) | copy-start | bytes 480004
  156.4 41.3 %copy-start.1 = (f32[128,200]{0,1:T(8,128)S(1)}, f32[128,200]{0,1:T(8,128)}, u32[]{:S(2)}) copy-start(f32[128,200]{0,1:T(8,128)} %param.7) | copy-start | bytes 307204
  156.4 41.3 %copy-start.2 = (f32[128,200]{0,1:T(8,128)S(1)}, f32[128,200]{0,1:T(8,128)}, u32[]{:S(2)}) copy-start(f32[128,200]{0,1:T(8,128)} %param.8) | copy-start | bytes 307204
  197.6 5.9 %collective-permute-start.2 = (f32[128,200]{0,1:T(8,128)S(1)}, f32[128,200]{0,1:T(8,128)S(1)}, u32[]{:S(2)}, u32[]{:S(2)}) collective-permute-start(f32[128,200]{0,1:T(8,128)S(1)} %collective-permute-done.1), channel_id=1, source_target_pairs={{0,1},{1,2},{2,3},{3,4},{4,5},{5,6},{6,7},{7,0},{8,9},{9,10},{10,1... | collective-permute-start | bytes 307208 | tf_op jit(solution)/shard_map/ppermute | solution.py:15
  203.6 18.6 %collective-permute-start.3 = (f32[128,200]{0,1:T(8,128)S(1)}, f32[128,200]{0,1:T(8,128)S(1)}, u32[]{:S(2)}, u32[]{:S(2)}) collective-permute-start(f32[128,200]{0,1:T(8,128)S(1)} %collective-permute-done.2), channel_id=1, source_target_pairs={{0,1},{1,2},{2,3},{3,4},{4,5},{5,6},{6,7},{7,0},{8,9},{9,10},{10,1... | collective-permute-start | bytes 307208 | tf_op jit(solution)/shard_map/ppermute | solution.py:15
  219.9 4.5 %collective-permute-start.6 = (f32[128,200]{0,1:T(8,128)S(1)}, f32[128,200]{0,1:T(8,128)S(1)}, u32[]{:S(2)}, u32[]{:S(2)}) collective-permute-start(f32[128,200]{0,1:T(8,128)S(1)} %collective-permute-done.5), channel_id=1, source_target_pairs={{0,7},{1,0},{2,1},{3,2},{4,3},{5,4},{6,5},{7,6},{8,15},{9,8},{10,9... | collective-permute-start | bytes 307208 | tf_op jit(solution)/shard_map/ppermute | solution.py:17
  224.5 26.7 %copy-start.4 = (u32[32]{0:T(128)S(1)}, u32[32]{0:T(128)}, u32[]{:S(2)}) copy-start(u32[32]{0:T(128)} %constant.183) | copy-start | bytes 388
  224.5 30.3 %copy-start = (f32[3,200,1024]{2,1,0:T(8,128)S(1)}, f32[3,200,1024]{2,1,0:T(8,128)}, u32[]{:S(2)}) copy-start(f32[3,200,1024]{2,1,0:T(8,128)} %param.6) | copy-start | bytes 7372804
  247.8 6.9 %collective-permute-start.7 = (f32[200,42]{0,1:T(8,128)S(1)}, f32[200,42]{0,1:T(8,128)S(1)}, u32[]{:S(2)}, u32[]{:S(2)}) collective-permute-start(f32[200,42]{0,1:T(8,128)S(1)} %slice.74), channel_id=1, source_target_pairs={{0,8},{8,16},{16,24},{1,9},{9,17},{17,25},{2,10},{10,18},{18,26},{... | collective-permute-start | bytes 100808
Sparse Core Ops, SparseCore 0:
  16.8 125.6 all-reduce.7
